TPU v7x, 32 devices: a whole 2x2x4 slice. The times are simulated.
32 devices in a mesh: day: 4 (over z), dom: 8 (over y, x, core).
Axes of the slice: x: 2, y: 2, z: 4, core: 2. Of those that a mesh axis runs over, the one named last changes fastest.
Arguments:
- node_states: bfloat16 [16, 2048, 256], P('day', 'dom'), may hold values from -12 to 12
- edge_source: int32 [16, 8192], P('day', 'dom'), may hold values from 0 to 383
- edge_target: int32 [16, 8192], P('day', 'dom'), may hold values from 0 to 255
- halo_rows: int32 [16, 1024], P('day', 'dom'), may hold values from 0 to 255
- halo_count: int32 [16, 8], P('day', 'dom'), may hold values from 1 to 128, 640 in all within a row
- w_message: bfloat16 [256, 256], replicated, may hold values from -0.375 to 0.375
- w_query: bfloat16 [256, 256], replicated, may hold values from -1 to 1, as said below
- w_key: bfloat16 [256, 256], replicated, may hold values from -1 to 1, as said below
- w_value: bfloat16 [256, 256], replicated, may hold values from -0.375 to 0.375
- cotangent: bfloat16 [16, 8, 4, 64, 256], P(None, 'dom', 'day'), may hold values from -6 to 6
Outputs:
- state_grad: float32 [16, 2048, 256], P('day', 'dom')
- grad_message: float32 [256, 256], replicated
- grad_query: float32 [256, 256], replicated
- grad_key: float32 [256, 256], replicated
- grad_value: float32 [256, 256], replicated
Inputs may be any that keep to these rules, and one draw needn't show every extreme that they name: `edge_source`: indices of the extended rows: below 256 a partition's own account, from 256 on a received halo slot. `halo_rows`: rows of the sending partition's own block; repeats allowed. `halo_count`: on every day some partition has all 128 slots live. `w_query`: entries of order 256 ** -0.5. `w_key`: entries of order 256 ** -0.5.
All inputs are finite; a program needn't handle non-finite values. No bound on the sum of `halo_count` on one device may be relied on, other than what follows from the above.
Results may differ from a plain program's by a relative error of at most 0.004.
The roundings to bfloat16 on the way count: a program that leaves them out, or rounds other values in their place, can miss the bound.
Values may be sent and summed in bfloat16 or wider, within the bound.
No kernel may reach another device: no remote copies, remote signals or barrier semaphores. Data moves between devices by JAX's collectives and lax.ppermute only.
A program may use at most 64 MiB of HBM per device.

v0:
```python
import jax
import jax.numpy as jnp
from jax import lax
from jax.sharding import PartitionSpec as P

HEADS = 4


def from_behind(value, axis, steps):
    count = lax.axis_size(axis)
    pairs = [(source, (source + steps) % count) for source in range(count)]
    return lax.ppermute(value, axis, pairs)


def adjacency(sources, targets, count_rows, total_rows):
    target_hot = (targets[:, None] == jnp.arange(count_rows, dtype=jnp.int32)[None, :]).astype(
        jnp.bfloat16
    )
    source_hot = (sources[:, None] == jnp.arange(total_rows, dtype=jnp.int32)[None, :]).astype(
        jnp.bfloat16
    )
    counts = lax.dot_general(
        target_hot, source_hot, (((0,), (0,)), ((), ())), preferred_element_type=jnp.float32
    )
    return counts.astype(jnp.bfloat16)


def gnn_forward(states, received, adjacent, w_message):
    extended = jnp.concatenate([states, received], axis=0)
    neighbours = jnp.dot(adjacent, extended, preferred_element_type=jnp.float32)
    counted = jnp.sum(adjacent.astype(jnp.float32), axis=1)
    inverse = 1.0 / (counted + 1.0)
    aggregate = ((states.astype(jnp.float32) + neighbours) * inverse[:, None]).astype(jnp.bfloat16)
    preact = jnp.dot(aggregate, w_message, preferred_element_type=jnp.float32)
    hidden = (states.astype(jnp.float32) + jax.nn.silu(preact)).astype(jnp.bfloat16)
    return (aggregate, preact, inverse, hidden)


def gnn_backward(upstream, aggregate, preact, inverse, adjacent, w_message):
    count_rows = aggregate.shape[0]
    up_float = upstream.astype(jnp.float32)
    sigmoid_val = jax.nn.sigmoid(preact)
    pre_grad = (up_float * sigmoid_val * (1.0 + preact * (1.0 - sigmoid_val))).astype(jnp.bfloat16)
    message_part = lax.dot_general(
        aggregate, pre_grad, (((0,), (0,)), ((), ())), preferred_element_type=jnp.float32
    )
    agg_grad = lax.dot_general(
        pre_grad, w_message, (((1,), (1,)), ((), ())), preferred_element_type=jnp.float32
    )
    term_grad = agg_grad * inverse[:, None]
    ext_grad = lax.dot_general(
        adjacent.astype(jnp.float32),
        term_grad,
        (((0,), (0,)), ((), ())),
        precision=lax.Precision.HIGHEST,
        preferred_element_type=jnp.float32,
    )
    local_grad = up_float + term_grad + ext_grad[:count_rows]
    halo_grad = ext_grad[count_rows:].astype(jnp.bfloat16)
    return (message_part, local_grad, halo_grad)


def attend(states, upstream, w_query, w_key, w_value):
    steps_all, nodes_here, width = states.shape
    head_dim = width // HEADS
    scale_factor = head_dim ** (-0.5)
    flat = states.reshape(steps_all * nodes_here, width)

    def project(weight):
        return jnp.dot(flat, weight, preferred_element_type=jnp.float32).astype(jnp.bfloat16)

    def splitter(matrix):
        return matrix.reshape(steps_all, nodes_here, HEADS, head_dim).astype(jnp.float32)

    queries = project(w_query)
    key_rows = project(w_key)
    value_rows = project(w_value)
    query_f = splitter(queries)
    key_f = splitter(key_rows)
    value_f = splitter(value_rows)
    scores = jnp.einsum("tnhd,snhd->nhts", query_f, key_f) * scale_factor
    causal = jnp.arange(steps_all)[:, None] >= jnp.arange(steps_all)[None, :]
    scores = jnp.where(causal, scores, -jnp.inf)
    highest = jnp.max(scores, axis=-1, keepdims=True)
    exponent = jnp.exp(scores - highest)
    probs = exponent / jnp.sum(exponent, axis=-1, keepdims=True)
    probs_low = probs.astype(jnp.bfloat16).astype(jnp.float32)
    up_heads = splitter(upstream)
    value_grad = jnp.einsum("nhts,tnhd->snhd", probs_low, up_heads).astype(jnp.bfloat16)
    prob_grad = jnp.einsum("tnhd,snhd->nhts", up_heads, value_f)
    score_grad = (
        probs * (prob_grad - jnp.sum(prob_grad * probs, axis=-1, keepdims=True)) * scale_factor
    ).astype(jnp.bfloat16)
    score_f = score_grad.astype(jnp.float32)
    query_grad = jnp.einsum("nhts,snhd->tnhd", score_f, key_f).astype(jnp.bfloat16)
    key_grad = jnp.einsum("nhts,tnhd->snhd", score_f, query_f).astype(jnp.bfloat16)
    query_flat = query_grad.reshape(steps_all * nodes_here, width)
    key_flat = key_grad.reshape(steps_all * nodes_here, width)
    value_flat = value_grad.reshape(steps_all * nodes_here, width)

    def weight_grad(grad_rows):
        return lax.dot_general(
            flat, grad_rows, (((0,), (0,)), ((), ())), preferred_element_type=jnp.float32
        )

    def input_grad(grad_rows, weight):
        return lax.dot_general(
            grad_rows, weight, (((1,), (1,)), ((), ())), preferred_element_type=jnp.float32
        )

    back = upstream.reshape(steps_all * nodes_here, width).astype(jnp.float32)
    back = (
        back
        + input_grad(query_flat, w_query)
        + input_grad(key_flat, w_key)
        + input_grad(value_flat, w_value)
    )
    back = back.astype(jnp.bfloat16).reshape(steps_all, nodes_here, width)
    return ((weight_grad(query_flat), weight_grad(key_flat), weight_grad(value_flat)), back)


def local(
    node_states,
    edge_source,
    edge_target,
    halo_rows,
    halo_count,
    w_message,
    w_query,
    w_key,
    w_value,
    cotangent,
):
    days_local, node_local, width = node_states.shape
    halo_slots = halo_rows.shape[1]
    live = jnp.arange(halo_slots)[None, :] < halo_count
    picked = jnp.take_along_axis(node_states, halo_rows[:, :, None], axis=1)
    sent = jnp.where(live[:, :, None], picked, jnp.zeros_like(picked))
    received = from_behind(sent, "dom", 1)

    def forward_one(items):
        adjacent = adjacency(items[2], items[3], node_local, node_local + halo_slots)
        aggregate, preact, inverse, hidden = gnn_forward(items[0], items[1], adjacent, w_message)
        return (aggregate, preact, inverse, hidden, adjacent)

    aggregate, preact, inverse, hidden, adjacent = lax.map(
        forward_one, (node_states, received, edge_source, edge_target)
    )
    node_major = lax.all_to_all(hidden, "day", split_axis=1, concat_axis=0, tiled=True)
    upstream = cotangent.reshape(cotangent.shape[0], -1, width)
    attn_grads, back = attend(node_major, upstream, w_query, w_key, w_value)
    back_days = lax.all_to_all(back, "day", split_axis=0, concat_axis=1, tiled=True)

    def backward_one(items):
        return gnn_backward(items[0], items[1], items[2], items[3], items[4], w_message)

    message_parts, local_grad, halo_grad = lax.map(
        backward_one, (back_days, aggregate, preact, inverse, adjacent)
    )
    grad_message = jnp.sum(message_parts, axis=0)
    returned = from_behind(halo_grad, "dom", -1)
    slot_hot = jnp.logical_and(
        halo_rows[:, :, None] == jnp.arange(node_local, dtype=jnp.int32)[None, None, :],
        live[:, :, None],
    ).astype(jnp.bfloat16)
    scattered = jnp.einsum("dsn,dsh->dnh", slot_hot, returned, preferred_element_type=jnp.float32)
    state_grad = local_grad + scattered
    grad_message, grad_query, grad_key, grad_value = lax.psum(
        (grad_message, attn_grads[0], attn_grads[1], attn_grads[2]), ("day", "dom")
    )
    return (state_grad, grad_message, grad_query, grad_key, grad_value)


def solution(mesh):
    return jax.shard_map(
        local,
        mesh=mesh,
        in_specs=(
            P("day", "dom", None),
            P("day", "dom"),
            P("day", "dom"),
            P("day", "dom"),
            P("day", "dom"),
            P(),
            P(),
            P(),
            P(),
            P(None, "dom", "day", None, None),
        ),
        out_specs=(P("day", "dom", None), P(), P(), P(), P()),
        check_vma=False,
    )
```

profile of v0, /device:TPU:0, one launch (start us, length us, event | category | flops | bytes accessed | tf_op | source)
XLA Modules:
  0.0 277.3 jit_solution(9602864403409959612)
XLA Ops:
  8.7 7.0 %gather_fusion = bf16[512,256]{1,0:T(8,128)(2,1)S(1)} fusion(bf16[4,256,256]{2,1,0:T(8,128)(2,1)} %param.14, s32[512]{0:T(512)S(1)} %fusion.70), kind=kCustom, calls=%fused_computation | custom fusion | bytes 528384 | tf_op jit(solution)/shard_map/jit(take_along_axis)/gather | solution.py:137
  16.4 6.9 %collective-permute-done = bf16[4,128,256]{2,1,0:T(8,128)(2,1)S(1)} collective-permute-done((bf16[4,128,256]{2,1,0:T(8,128)(2,1)S(1)}, bf16[4,128,256]{2,1,0:T(8,128)(2,1)S(1)}, u32[]{:S(2)}, u32[]{:S(2)}) %collective-permute-start) | collective-permute-done | bytes 262176 | tf_op jit(solution)/shard_map/ppermute | solution.py:12
  23.4 12.2 %while.34 = (s32[]{:T(128)}, bf16[4,256,256]{2,1,0:T(8,128)(2,1)S(1)}, f32[4,256,256]{2,1,0:T(8,128)S(1)}, f32[4,256]{1,0:T(4,128)S(1)}, bf16[4,256,256]{2,1,0:T...) while((s32[]{:T(128)}, ...), condition=%wide.region_2.3_spmd.clone, body=%wide.region_0.2_spmd.sunk.clone | while | flops 287277312 | bytes 3111561 | solution.py:146
  36.9 5.6 %all-to-all-start = ((bf16[4,256,256]{2,0,1:T(4,128)(2,1)}), bf16[4,256,256]{2,0,1:T(4,128)(2,1)S(1)}, u32[]{:S(2)}, u32[]{:S(2)}) async-start(bf16[4,256,256]{2,0,1:T(4,128)(2,1)} %copy.52), calls=%async_computation | async-start | bytes 1048576 | tf_op jit(solution)/shard_map/all_to_all | solution.py:149
  42.9 12.5 %all-to-all-done = bf16[4,256,256]{2,0,1:T(4,128)(2,1)S(1)} async-done(((bf16[4,256,256]{2,0,1:T(4,128)(2,1)}), bf16[4,256,256]{2,0,1:T(4,128)(2,1)S(1)}, u32[]{:S(2)}, u32[]{:S(2)}) %all-to-all-start) | async-done | bytes 524320 | tf_op jit(solution)/shard_map/all_to_all | solution.py:149
  55.8 1.4 reshape.100
  57.5 1.4 reshape.99
  59.6 2.6 fusion.52
  62.3 4.9 %fusion.77 = (f32[64,4,16]{2,1,0:T(4,128)S(1)}, f32[64,4,16,16]{2,3,1,0:T(8,128)}) fusion(pred[16,16]{0,1:T(8,128)(4,1)S(1)} %iota_compare_fusion.7, bf16[16,64,4,64]{3,2,1,0:T(4,128)(2,1)} %reshape.99, bf16[16,64,4,64]{3,2,1,0:T(4,128)(2,1)} %reshape.100), kind=kOutput, calls=%fused_computation.119 | convolution fusion | flops 8650767 | bytes 1327360 | tf_op jit(solution)/shard_map/sub | solution.py:85
  67.2 5.8 %fusion.50 = bf16[16,64,4,64]{3,0,2,1:T(8,128)(2,1)} fusion(f32[64,4,16,16]{3,2,1,0:T(8,128)} %fusion.52, bf16[16,64,4,64]{3,2,1,0:T(4,128)(2,1)S(1)} %copy-done.5, f32[64,4,16,16]{2,3,1,0:T(8,128)} %get-tuple-element.183, f32[64,4,16]{2,1,0:T(4,128)S(1)} %get-tuple-element.182), kind=kOutput, calls=%fused_computation.78 | convolution fusion | flops 9113615 | bytes 1589248 | tf_op jit(solution)/shard_map/nhts,tnhd->snhd/dot_general | solution.py:96
  73.0 6.1 %fusion.48 = bf16[16,64,4,64]{3,0,2,1:T(8,128)(2,1)} fusion(f32[64,4,16,16]{3,2,1,0:T(8,128)} %fusion.52, bf16[16,64,4,64]{3,2,1,0:T(4,128)(2,1)} %reshape.99, f32[64,4,16,16]{2,3,1,0:T(8,128)} %get-tuple-element.183, f32[64,4,16]{2,1,0:T(4,128)S(1)} %get-tuple-element.182), kind=kOutput, calls=%fused_computation.76 | convolution fusion | flops 9113615 | bytes 1589248 | tf_op jit(solution)/shard_map/nhts,snhd->tnhd/dot_general | solution.py:95
  79.2 3.5 %fusion.49 = bf16[16,64,4,64]{3,0,2,1:T(8,128)(2,1)} fusion(bf16[16,64,4,64]{3,2,1,0:T(4,128)(2,1)S(1)} %reshape_reshape.4, f32[64,4,16,16]{2,3,1,0:T(8,128)} %get-tuple-element.183, f32[64,4,16]{2,1,0:T(4,128)} %copy-done.13), kind=kOutput, calls=%fused_computation.77 | convolution fusion | flops 8781824 | bytes 1327104 | tf_op jit(solution)/shard_map/nhts,tnhd->snhd/dot_general | solution.py:89
  82.7 1.7 copy.63
  85.2 3.1 %copy.61 = bf16[16,64,4,64]{1,0,3,2:T(8,128)(2,1)S(1)} copy(bf16[16,64,4,64]{3,0,2,1:T(8,128)(2,1)} %fusion.48) | data formatting | bytes 1048576 | tf_op jit(solution)/shard_map/convert_element_type | solution.py:95
  89.0 2.9 %copy.65 = bf16[16,64,4,64]{1,0,3,2:T(8,128)(2,1)S(1)} copy(bf16[16,64,4,64]{3,0,2,1:T(8,128)(2,1)} %fusion.49) | data formatting | bytes 1048576 | tf_op jit(solution)/shard_map/convert_element_type | solution.py:89
  92.7 1.4 convolution_add_fusion.3
  95.6 3.5 %all-to-all-start.1 = ((bf16[16,64,256]{2,1,0:T(8,128)(2,1)}), bf16[16,64,256]{2,1,0:T(8,128)(2,1)S(1)}, u32[]{:S(2)}, u32[]{:S(2)}) async-start(bf16[16,64,256]{2,1,0:T(8,128)(2,1)} %bitcast.30), calls=%async_computation.1 | async-start | bytes 1048576 | tf_op jit(solution)/shard_map/all_to_all | solution.py:152
  101.3 10.9 %all-to-all-done.1 = bf16[16,64,256]{2,1,0:T(8,128)(2,1)S(1)} async-done(((bf16[16,64,256]{2,1,0:T(8,128)(2,1)}), bf16[16,64,256]{2,1,0:T(8,128)(2,1)S(1)}, u32[]{:S(2)}, u32[]{:S(2)}) %all-to-all-start.1) | async-done | bytes 524320 | tf_op jit(solution)/shard_map/all_to_all | solution.py:152
  113.1 18.6 %while.35 = (s32[]{:T(128)}, f32[4,256,256]{2,1,0:T(8,128)S(1)}, f32[4,256,256]{2,1,0:T(8,128)S(1)}, bf16[4,128,256]{2,1,0:T(8,128)(2,1)}, bf16[4,256,256]{2,1,0...) while((s32[]{:T(128)}, f32[4,256,256]{2,1,0:T(8,128)S(1)}, ...), condition=%wide.region_7.8_spmd.clone, body=%wide.region_6.7_spmd.sunk.clone | while | flops 370671616 | bytes 5576841 | solution.py:157
  114.5 1.3 fusion.149
  116.5 1.3 fusion.148
  119.1 1.3 fusion.149
  123.8 1.3 fusion.149
  125.8 1.3 fusion.148
  128.4 1.3 fusion.149
  133.7 2.3 collective-permute-done.1
  136.0 2.4 convolution_add_fusion.4
  138.5 125.3 %all-reduce.3.cloned.1.call-done = (f32[256,256]{1,0:T(8,128)}, f32[256,256]{1,0:T(8,128)}, f32[256,256]{1,0:T(8,128)}, f32[256,256]{1,0:T(8,128)}) async-done(((f32[256,256]{1,0:T(8,128)}, f32[256,256]{1,0:T(8,128)}, f32[256,256]{1,0:T(8,128)}, f32[256,256]{1,0:T(8,128)}), (f32[256,256]{1,0:T(8,128)}, f32[256,256]{1,0:T(8,128)}, f32[256,256]{1,0:T(8,128)}, ...) | async-done | bytes 1048592 | tf_op jit(solution)/shard_map/psum | solution.py:168
  263.8 1.7 copy.137
  265.5 1.7 copy.138
  267.1 1.7 copy.139
  268.8 1.7 copy.140
  (126 shorter events, 36.6 us)
Async XLA Ops:
  7.2 48.3 %copy-start = (bf16[256,256]{1,0:T(8,128)(2,1)S(1)}, bf16[256,256]{1,0:T(8,128)(2,1)}, u32[]{:S(2)}) copy-start(bf16[256,256]{1,0:T(8,128)(2,1)} %param.20) | copy-start | bytes 393220
  8.7 14.8 %copy-start.1 = (bf16[4,256,256]{2,1,0:T(8,128)(2,1)S(1)}, bf16[4,256,256]{2,1,0:T(8,128)(2,1)}, u32[]{:S(2)}) copy-start(bf16[4,256,256]{2,1,0:T(8,128)(2,1)} %param.14) | copy-start | bytes 1572868
  8.7 14.8 %copy-start.2 = (bf16[256,256]{1,0:T(8,128)(2,1)S(1)}, bf16[256,256]{1,0:T(8,128)(2,1)}, u32[]{:S(2)}) copy-start(bf16[256,256]{1,0:T(8,128)(2,1)} %param.19) | copy-start | bytes 393220
  15.9 7.4 %collective-permute-start = (bf16[4,128,256]{2,1,0:T(8,128)(2,1)S(1)}, bf16[4,128,256]{2,1,0:T(8,128)(2,1)S(1)}, u32[]{:S(2)}, u32[]{:S(2)}) collective-permute-start(bf16[4,128,256]{2,1,0:T(8,128)(2,1)S(1)} %select_select_fusion), channel_id=1, source_target_pairs={{0,1},{1,2},{2,3},{3,4},{4,5},{5,6},{6,7},{7,0},{8,9},{9,10},{10,1... | collective-permute-start | bytes 786440 | tf_op jit(solution)/shard_map/ppermute | solution.py:12
  35.6 1.2 copy-start.6
  35.6 19.8 %copy-start.12 = (bf16[4,256,256]{2,1,0:T(8,128)(2,1)}, bf16[4,256,256]{2,1,0:T(8,128)(2,1)S(1)}, u32[]{:S(2)}) copy-start(bf16[4,256,256]{2,1,0:T(8,128)(2,1)S(1)} %get-tuple-element.422) | copy-start | bytes 1572868
  35.6 6.8 %copy-start.4 = (bf16[16,1,1,64,256]{4,3,2,1,0:T(8,128)(2,1)S(1)}, bf16[16,1,1,64,256]{4,3,2,1,0:T(8,128)(2,1)}, u32[]{:S(2)}) copy-start(bf16[16,1,1,64,256]{4,3,2,1,0:T(8,128)(2,1)} %param.23) | copy-start | bytes 1572868
  36.9 18.5 %all-to-all-start = ((bf16[4,256,256]{2,0,1:T(4,128)(2,1)}), bf16[4,256,256]{2,0,1:T(4,128)(2,1)S(1)}, u32[]{:S(2)}, u32[]{:S(2)}) async-start(bf16[4,256,256]{2,0,1:T(4,128)(2,1)} %copy.52), calls=%async_computation | async-start | bytes 1048576 | tf_op jit(solution)/shard_map/all_to_all | solution.py:149
  55.4 1.8 copy-start.9
  55.8 3.1 %copy-start.8 = (bf16[256,256]{1,0:T(8,128)(2,1)S(1)}, bf16[256,256]{1,0:T(8,128)(2,1)}, u32[]{:S(2)}) copy-start(bf16[256,256]{1,0:T(8,128)(2,1)} %param.22) | copy-start | bytes 393220
  62.3 5.0 %copy-start.5 = (bf16[16,64,4,64]{3,2,1,0:T(4,128)(2,1)S(1)}, bf16[16,64,4,64]{3,2,1,0:T(4,128)(2,1)}, u32[]{:S(2)}) copy-start(bf16[16,64,4,64]{3,2,1,0:T(4,128)(2,1)} %reshape.100) | copy-start | bytes 1572868
  67.2 5.8 %copy-start.13 = (f32[64,4,16]{2,1,0:T(4,128)}, f32[64,4,16]{2,1,0:T(4,128)S(1)}, u32[]{:S(2)}) copy-start(f32[64,4,16]{2,1,0:T(4,128)S(1)} %get-tuple-element.182) | copy-start | bytes 49156
  79.2 3.5 %copy-start.7 = (bf16[16,64,4,64]{3,0,2,1:T(8,128)(2,1)S(1)}, bf16[16,64,4,64]{3,0,2,1:T(8,128)(2,1)}, u32[]{:S(2)}) copy-start(bf16[16,64,4,64]{3,0,2,1:T(8,128)(2,1)} %fusion.50) | copy-start | bytes 1572868
  92.7 1.5 copy-start.10
  95.6 16.5 %all-to-all-start.1 = ((bf16[16,64,256]{2,1,0:T(8,128)(2,1)}), bf16[16,64,256]{2,1,0:T(8,128)(2,1)S(1)}, u32[]{:S(2)}, u32[]{:S(2)}) async-start(bf16[16,64,256]{2,1,0:T(8,128)(2,1)} %bitcast.30), calls=%async_computation.1 | async-start | bytes 1048576 | tf_op jit(solution)/shard_map/all_to_all | solution.py:152
  99.1 164.7 %all-reduce.3.cloned.1.call-start = ((), (), s32[]{:S(2)}) async-start(), calls=%async_computation.2 | async-start | bytes 2097152 | tf_op jit(solution)/shard_map/psum | solution.py:168
  113.2 2.6 copy-start.3
  117.8 2.6 copy-start.3
  122.5 2.6 copy-start.3
  127.1 2.6 copy-start.3
  131.8 4.3 %copy-start.11 = (s32[4,128]{1,0:T(4,128)S(1)}, s32[4,128]{1,0:T(4,128)}, u32[]{:S(2)}) copy-start(s32[4,128]{1,0:T(4,128)} %param.17) | copy-start | bytes 6148
  131.8 4.3 %collective-permute-start.1 = (bf16[4,128,256]{2,1,0:T(8,128)(2,1)}, bf16[4,128,256]{2,1,0:T(8,128)(2,1)}, u32[]{:S(2)}, u32[]{:S(2)}) collective-permute-start(bf16[4,128,256]{2,1,0:T(8,128)(2,1)} %get-tuple-element.126), channel_id=1, source_target_pairs={{0,7},{1,0},{2,1},{3,2},{4,3},{5,4},{6,5},{7,6},{8,15},{9,8},{10,9... | collective-permute-start | bytes 786440 | tf_op jit(solution)/shard_map/ppermute | solution.py:12
Sparse Core Ops, SparseCore 0:
  133.8 129.9 all-reduce.2
where the time goes:
time: 278 us; the launch traced here: 277 us
  waiting for transfers between devices  158 us (57%)
  matrix products  53.5 us (19%)
  local copies, waits for them, and re-layouts  38.3 us (14%)
  between operations  14.4 us (5%)
  starting transfers between devices  9.7 us (3%)
  other arithmetic  3.06 us (1%)
    psum x1, waiting for transfers between devices, local(): lax.psum((grad_message, attn_grads[0], attn_grads[1], attn_grads[2]), ('d...  125 us
    all_to_all x1, waiting for transfers between devices, local(): lax.all_to_all(hidden, 'day', split_axis=1, concat_axis=0, tiled=True)  12.5 us
    all_to_all x1, waiting for transfers between devices, local(): lax.all_to_all(back, 'day', split_axis=0, concat_axis=1, tiled=True)  10.9 us
    ppermute x2, waiting for transfers between devices, from_behind(): return lax.ppermute(value, axis, pairs)  9.28 us
    gather x1, local copies, waits for them, and re-layouts, local(): picked = jnp.take_along_axis(node_states, halo_rows[:, :, None], axis=1)  7 us
    unnamed x30, local copies, waits for them, and re-layouts  6.74 us
    dot_general x1, matrix products, attend(): jnp.einsum('nhts,snhd->tnhd', score_f, key_f).astype(jnp.bfloat16)  6.14 us
    dot_general x1, matrix products, attend(): jnp.einsum('nhts,tnhd->snhd', score_f, query_f).astype(jnp.bfloat16)  5.79 us
  transfers between devices with their start and end apart: 5, of which 5 were waited for; matrix products, arithmetic and copies ran while one was open for 2% of the time, Pallas kernels for 0%

commit v1 on v0

--- a/solution.py
+++ b/solution.py
@@ -149,7 +149,9 @@
     node_major = lax.all_to_all(hidden, "day", split_axis=1, concat_axis=0, tiled=True)
     upstream = cotangent.reshape(cotangent.shape[0], -1, width)
     attn_grads, back = attend(node_major, upstream, w_query, w_key, w_value)
-    back_days = lax.all_to_all(back, "day", split_axis=0, concat_axis=1, tiled=True)
+    cells = jnp.split(back, lax.axis_size("day"), axis=0)
+    incoming = lax.all_to_all(jnp.stack(cells), "day", 0, 0)
+    back_days = jnp.concatenate(incoming, axis=1)
 
     def backward_one(items):
         return gnn_backward(items[0], items[1], items[2], items[3], items[4], w_message)

time: 278 us -> 279 us (level)
    unnamed x30 -> x26, local copies, waits for them, and re-layouts: 6.74 us -> 6.73 us
where the time goes in v1:
time: 279 us; the launch traced here: 278 us
  waiting for transfers between devices  158 us (57%)
  matrix products  52.5 us (19%)
  local copies, waits for them, and re-layouts  39.5 us (14%)
  between operations  14.4 us (5%)
  starting transfers between devices  9.7 us (3%)
  other arithmetic  3.92 us (1%)
    psum x1, waiting for transfers between devices, local(): lax.psum((grad_message, attn_grads[0], attn_grads[1], attn_grads[2]), ('d...  125 us
    all_to_all x1, waiting for transfers between devices, local(): lax.all_to_all(hidden, 'day', split_axis=1, concat_axis=0, tiled=True)  12.5 us
    all_to_all x1, waiting for transfers between devices, local(): incoming = lax.all_to_all(jnp.stack(cells), 'day', 0, 0)  10.9 us
    ppermute x2, waiting for transfers between devices, from_behind(): return lax.ppermute(value, axis, pairs)  9.29 us
    gather x1, local copies, waits for them, and re-layouts, local(): picked = jnp.take_along_axis(node_states, halo_rows[:, :, None], axis=1)  7 us
    unnamed x26, local copies, waits for them, and re-layouts  6.73 us
    dot_general x1, matrix products, attend(): jnp.einsum('nhts,tnhd->snhd', score_f, query_f).astype(jnp.bfloat16)  6.08 us
    dot_general x1, matrix products, attend(): jnp.einsum('nhts,snhd->tnhd', score_f, key_f).astype(jnp.bfloat16)  5.83 us
  transfers between devices with their start and end apart: 5, of which 5 were waited for; matrix products, arithmetic and copies ran while one was open for 2% of the time, Pallas kernels for 0%

profile of v1, /device:TPU:0, one launch (start us, length us, event | category | flops | bytes accessed | tf_op | source)
XLA Modules:
  0.0 278.3 jit_solution(8705375120052434309)
XLA Ops:
  8.7 7.0 %gather_fusion = bf16[512,256]{1,0:T(8,128)(2,1)S(1)} fusion(bf16[4,256,256]{2,1,0:T(8,128)(2,1)} %param.14, s32[512]{0:T(512)S(1)} %fusion.70), kind=kCustom, calls=%fused_computation | custom fusion | bytes 528384 | tf_op jit(solution)/shard_map/jit(take_along_axis)/gather | solution.py:137
  16.4 6.9 %collective-permute-done = bf16[4,128,256]{2,1,0:T(8,128)(2,1)S(1)} collective-permute-done((bf16[4,128,256]{2,1,0:T(8,128)(2,1)S(1)}, bf16[4,128,256]{2,1,0:T(8,128)(2,1)S(1)}, u32[]{:S(2)}, u32[]{:S(2)}) %collective-permute-start) | collective-permute-done | bytes 262176 | tf_op jit(solution)/shard_map/ppermute | solution.py:12
  23.4 12.1 %while.34 = (s32[]{:T(128)}, bf16[4,256,256]{2,1,0:T(8,128)(2,1)S(1)}, f32[4,256,256]{2,1,0:T(8,128)S(1)}, f32[4,256]{1,0:T(4,128)S(1)}, bf16[4,256,256]{2,1,0:T...) while((s32[]{:T(128)}, ...), condition=%wide.region_2.3_spmd.clone, body=%wide.region_0.2_spmd.sunk.clone | while | flops 287277312 | bytes 3111561 | solution.py:146
  36.8 5.6 %all-to-all-start = ((bf16[4,256,256]{2,0,1:T(4,128)(2,1)}), bf16[4,256,256]{2,0,1:T(4,128)(2,1)S(1)}, u32[]{:S(2)}, u32[]{:S(2)}) async-start(bf16[4,256,256]{2,0,1:T(4,128)(2,1)} %copy.52), calls=%async_computation | async-start | bytes 1048576 | tf_op jit(solution)/shard_map/all_to_all | solution.py:149
  42.9 12.5 %all-to-all-done = bf16[4,256,256]{2,0,1:T(4,128)(2,1)S(1)} async-done(((bf16[4,256,256]{2,0,1:T(4,128)(2,1)}), bf16[4,256,256]{2,0,1:T(4,128)(2,1)S(1)}, u32[]{:S(2)}, u32[]{:S(2)}) %all-to-all-start) | async-done | bytes 524320 | tf_op jit(solution)/shard_map/all_to_all | solution.py:149
  55.8 1.4 reshape.111
  57.5 1.4 reshape.112
  59.6 2.6 fusion.52
  62.2 4.9 %fusion.78 = (f32[64,4,16]{2,1,0:T(4,128)S(1)}, f32[64,4,16,16]{2,3,1,0:T(8,128)}) fusion(pred[16,16]{0,1:T(8,128)(4,1)S(1)} %iota_compare_fusion.7, bf16[16,64,4,64]{3,2,1,0:T(4,128)(2,1)} %reshape.111, bf16[16,64,4,64]{3,2,1,0:T(4,128)(2,1)} %reshape.112), kind=kOutput, calls=%fused_computation.121 | convolution fusion | flops 8650767 | bytes 1327360 | tf_op jit(solution)/shard_map/sub | solution.py:85
  67.1 6.1 %fusion.50 = bf16[16,64,4,64]{3,0,2,1:T(8,128)(2,1)} fusion(f32[64,4,16,16]{3,2,1,0:T(8,128)} %fusion.52, bf16[16,64,4,64]{3,2,1,0:T(4,128)(2,1)} %reshape.112, f32[64,4,16,16]{2,3,1,0:T(8,128)} %get-tuple-element.187, f32[64,4,16]{2,1,0:T(4,128)S(1)} %get-tuple-element.186), kind=kOutput, calls=%fused_computation.78 | convolution fusion | flops 9113615 | bytes 1589248 | tf_op jit(solution)/shard_map/nhts,tnhd->snhd/dot_general | solution.py:96
  73.2 5.8 %fusion.48 = bf16[16,64,4,64]{3,0,2,1:T(8,128)(2,1)} fusion(f32[64,4,16,16]{3,2,1,0:T(8,128)} %fusion.52, bf16[16,64,4,64]{3,2,1,0:T(4,128)(2,1)S(1)} %copy-done.5, f32[64,4,16,16]{2,3,1,0:T(8,128)} %get-tuple-element.187, f32[64,4,16]{2,1,0:T(4,128)S(1)} %get-tuple-element.186), kind=kOutput, calls=%fused_computation.76 | convolution fusion | flops 9113615 | bytes 1589248 | tf_op jit(solution)/shard_map/nhts,snhd->tnhd/dot_general | solution.py:95
  79.0 3.5 %fusion.49 = bf16[16,64,4,64]{3,0,2,1:T(8,128)(2,1)} fusion(bf16[16,64,4,64]{3,2,1,0:T(4,128)(2,1)S(1)} %reshape_reshape.4, f32[64,4,16,16]{2,3,1,0:T(8,128)} %get-tuple-element.187, f32[64,4,16]{2,1,0:T(4,128)S(1)} %get-tuple-element.186), kind=kOutput, calls=%fused_computation.77 | convolution fusion | flops 8781824 | bytes 1327104 | tf_op jit(solution)/shard_map/nhts,tnhd->snhd/dot_general | solution.py:89
  82.5 2.9 %copy.63 = bf16[16,64,4,64]{1,0,3,2:T(8,128)(2,1)S(1)} copy(bf16[16,64,4,64]{3,0,2,1:T(8,128)(2,1)} %fusion.50) | data formatting | bytes 1048576 | tf_op jit(solution)/shard_map/convert_element_type | solution.py:96
  86.1 3.1 %copy.61 = bf16[16,64,4,64]{1,0,3,2:T(8,128)(2,1)S(1)} copy(bf16[16,64,4,64]{3,0,2,1:T(8,128)(2,1)} %fusion.48) | data formatting | bytes 1048576 | tf_op jit(solution)/shard_map/convert_element_type | solution.py:95
  89.9 2.9 %copy.65 = bf16[16,64,4,64]{1,0,3,2:T(8,128)(2,1)S(1)} copy(bf16[16,64,4,64]{3,0,2,1:T(8,128)(2,1)} %fusion.49) | data formatting | bytes 1048576 | tf_op jit(solution)/shard_map/convert_element_type | solution.py:89
  93.6 1.4 convolution_add_fusion.3
  96.7 3.5 %all-to-all-start.1 = ((bf16[4,4,64,256]{3,2,1,0:T(8,128)(2,1)}), bf16[4,4,64,256]{3,2,1,0:T(8,128)(2,1)S(1)}, u32[]{:S(2)}, u32[]{:S(2)}) async-start(bf16[4,4,64,256]{3,2,1,0:T(8,128)(2,1)} %pad_maximum_fusion), calls=%async_computation.1 | async-start | bytes 1048576 | tf_op jit(solution)/shard_map/all_to_all | solution.py:153
  102.3 10.9 %all-to-all-done.1 = bf16[4,4,64,256]{3,2,1,0:T(8,128)(2,1)S(1)} async-done(((bf16[4,4,64,256]{3,2,1,0:T(8,128)(2,1)}), bf16[4,4,64,256]{3,2,1,0:T(8,128)(2,1)S(1)}, u32[]{:S(2)}, u32[]{:S(2)}) %all-to-all-start.1) | async-done | bytes 524320 | tf_op jit(solution)/shard_map/all_to_all | solution.py:153
  114.2 18.6 %while.35 = (s32[]{:T(128)}, f32[4,256,256]{2,1,0:T(8,128)S(1)}, f32[4,256,256]{2,1,0:T(8,128)S(1)}, bf16[4,128,256]{2,1,0:T(8,128)(2,1)}, bf16[4,256,256]{2,1,0...) while((s32[]{:T(128)}, f32[4,256,256]{2,1,0:T(8,128)S(1)}, ...), condition=%wide.region_7.8_spmd.clone, body=%wide.region_6.7_spmd.sunk.clone | while | flops 370671616 | bytes 5576841 | solution.py:159
  115.5 1.3 fusion.150
  122.2 1.3 fusion.149
  124.8 1.3 fusion.150
  126.9 1.3 fusion.149
  129.5 1.3 fusion.150
  131.5 1.3 fusion.149
  134.7 2.4 collective-permute-done.1
  137.1 2.4 convolution_add_fusion.4
  139.5 125.3 %all-reduce.3.cloned.1.call-done = (f32[256,256]{1,0:T(8,128)}, f32[256,256]{1,0:T(8,128)}, f32[256,256]{1,0:T(8,128)}, f32[256,256]{1,0:T(8,128)}) async-done(((f32[256,256]{1,0:T(8,128)}, f32[256,256]{1,0:T(8,128)}, f32[256,256]{1,0:T(8,128)}, f32[256,256]{1,0:T(8,128)}), (f32[256,256]{1,0:T(8,128)}, f32[256,256]{1,0:T(8,128)}, f32[256,256]{1,0:T(8,128)}, ...) | async-done | bytes 1048592 | tf_op jit(solution)/shard_map/psum | solution.py:170
  264.8 1.7 copy.137
  266.5 1.7 copy.138
  268.1 1.7 copy.139
  269.8 1.7 copy.140
  (124 shorter events, 36.7 us)
Async XLA Ops:
  7.2 50.0 %copy-start = (bf16[256,256]{1,0:T(8,128)(2,1)S(1)}, bf16[256,256]{1,0:T(8,128)(2,1)}, u32[]{:S(2)}) copy-start(bf16[256,256]{1,0:T(8,128)(2,1)} %param.20) | copy-start | bytes 393220
  8.7 14.8 %copy-start.1 = (bf16[4,256,256]{2,1,0:T(8,128)(2,1)S(1)}, bf16[4,256,256]{2,1,0:T(8,128)(2,1)}, u32[]{:S(2)}) copy-start(bf16[4,256,256]{2,1,0:T(8,128)(2,1)} %param.14) | copy-start | bytes 1572868
  8.7 14.8 %copy-start.2 = (bf16[256,256]{1,0:T(8,128)(2,1)S(1)}, bf16[256,256]{1,0:T(8,128)(2,1)}, u32[]{:S(2)}) copy-start(bf16[256,256]{1,0:T(8,128)(2,1)} %param.19) | copy-start | bytes 393220
  15.9 7.4 %collective-permute-start = (bf16[4,128,256]{2,1,0:T(8,128)(2,1)S(1)}, bf16[4,128,256]{2,1,0:T(8,128)(2,1)S(1)}, u32[]{:S(2)}, u32[]{:S(2)}) collective-permute-start(bf16[4,128,256]{2,1,0:T(8,128)(2,1)S(1)} %select_select_fusion), channel_id=1, source_target_pairs={{0,1},{1,2},{2,3},{3,4},{4,5},{5,6},{6,7},{7,0},{8,9},{9,10},{10,1... | collective-permute-start | bytes 786440 | tf_op jit(solution)/shard_map/ppermute | solution.py:12
  35.6 1.2 copy-start.6
  35.6 19.8 %copy-start.11 = (bf16[4,256,256]{2,1,0:T(8,128)(2,1)}, bf16[4,256,256]{2,1,0:T(8,128)(2,1)S(1)}, u32[]{:S(2)}) copy-start(bf16[4,256,256]{2,1,0:T(8,128)(2,1)S(1)} %get-tuple-element.426) | copy-start | bytes 1572868
  35.6 6.8 %copy-start.4 = (bf16[16,1,1,64,256]{4,3,2,1,0:T(8,128)(2,1)S(1)}, bf16[16,1,1,64,256]{4,3,2,1,0:T(8,128)(2,1)}, u32[]{:S(2)}) copy-start(bf16[16,1,1,64,256]{4,3,2,1,0:T(8,128)(2,1)} %param.23) | copy-start | bytes 1572868
  36.8 18.5 %all-to-all-start = ((bf16[4,256,256]{2,0,1:T(4,128)(2,1)}), bf16[4,256,256]{2,0,1:T(4,128)(2,1)S(1)}, u32[]{:S(2)}, u32[]{:S(2)}) async-start(bf16[4,256,256]{2,0,1:T(4,128)(2,1)} %copy.52), calls=%async_computation | async-start | bytes 1048576 | tf_op jit(solution)/shard_map/all_to_all | solution.py:149
  42.5 13.0 %copy-start.8 = (bf16[256,256]{1,0:T(8,128)(2,1)S(1)}, bf16[256,256]{1,0:T(8,128)(2,1)}, u32[]{:S(2)}) copy-start(bf16[256,256]{1,0:T(8,128)(2,1)} %param.21) | copy-start | bytes 393220
  55.8 3.1 %copy-start.7 = (bf16[256,256]{1,0:T(8,128)(2,1)S(1)}, bf16[256,256]{1,0:T(8,128)(2,1)}, u32[]{:S(2)}) copy-start(bf16[256,256]{1,0:T(8,128)(2,1)} %param.22) | copy-start | bytes 393220
  67.1 6.1 %copy-start.5 = (bf16[16,64,4,64]{3,2,1,0:T(4,128)(2,1)S(1)}, bf16[16,64,4,64]{3,2,1,0:T(4,128)(2,1)}, u32[]{:S(2)}) copy-start(bf16[16,64,4,64]{3,2,1,0:T(4,128)(2,1)} %reshape.111) | copy-start | bytes 1572868
  93.6 1.5 copy-start.9
  96.7 16.5 %all-to-all-start.1 = ((bf16[4,4,64,256]{3,2,1,0:T(8,128)(2,1)}), bf16[4,4,64,256]{3,2,1,0:T(8,128)(2,1)S(1)}, u32[]{:S(2)}, u32[]{:S(2)}) async-start(bf16[4,4,64,256]{3,2,1,0:T(8,128)(2,1)} %pad_maximum_fusion), calls=%async_computation.1 | async-start | bytes 1048576 | tf_op jit(solution)/shard_map/all_to_all | solution.py:153
  100.1 164.6 %all-reduce.3.cloned.1.call-start = ((), (), s32[]{:S(2)}) async-start(), calls=%async_computation.2 | async-start | bytes 2097152 | tf_op jit(solution)/shard_map/psum | solution.py:170
  114.2 2.6 copy-start.3
  118.9 2.6 copy-start.3
  123.5 2.6 copy-start.3
  128.2 2.6 copy-start.3
  132.8 4.3 %copy-start.10 = (s32[4,128]{1,0:T(4,128)S(1)}, s32[4,128]{1,0:T(4,128)}, u32[]{:S(2)}) copy-start(s32[4,128]{1,0:T(4,128)} %param.17) | copy-start | bytes 6148
  132.8 4.3 %collective-permute-start.1 = (bf16[4,128,256]{2,1,0:T(8,128)(2,1)}, bf16[4,128,256]{2,1,0:T(8,128)(2,1)}, u32[]{:S(2)}, u32[]{:S(2)}) collective-permute-start(bf16[4,128,256]{2,1,0:T(8,128)(2,1)} %get-tuple-element.126), channel_id=1, source_target_pairs={{0,7},{1,0},{2,1},{3,2},{4,3},{5,4},{6,5},{7,6},{8,15},{9,8},{10,9... | collective-permute-start | bytes 786440 | tf_op jit(solution)/shard_map/ppermute | solution.py:12
Sparse Core Ops, SparseCore 0:
  134.9 129.8 all-reduce.2
